TPU v7x, 32 devices: a whole 2x2x4 slice. The times are simulated.
32 devices in a mesh: grp: 2 (over y), wide: 4 (over z), col: 2 (over x), inc: 2 (over core).
Axes of the slice: x: 2, y: 2, z: 4, core: 2. Of those that a mesh axis runs over, the one named last changes fastest.
Arguments:
- values_in: bfloat16 [32, 64, 256, 512], P(('grp', 'col'), 'inc', 'wide'), parts along dimension 0, may hold values from -6 to 6
- shock_load: float32 [32], P(('grp', 'col')), parts along dimension 0, may hold values from -4 to 4
- price_field: float32 [128, 256, 512], P(('grp', 'inc'), 'wide'), parts along dimension 0, may hold values from -6 to 6
- rate_liquid: float32 [128, 256, 512], P(('grp', 'inc'), 'wide'), parts along dimension 0, may hold values from 0.05 to 0.5
- rate_illiquid: float32 [128, 256, 512], P(('grp', 'inc'), 'wide'), parts along dimension 0, may hold values from 0.05 to 0.5
- mask_liquid: int32 [128, 256, 512], P(('grp', 'inc'), 'wide'), parts along dimension 0, may hold values 0 or 1
- mask_illiquid: int32 [128, 256, 512], P(('grp', 'inc'), 'wide'), parts along dimension 0, may hold values 0 or 1
- jump_inverse: float32 [128, 64], P('grp'), parts along dimension 0, may hold values from -0.07 to 0.87
- coef_liquid: int32 [4096], replicated, may hold values from 0 to 127, as said below
- coef_illiquid: int32 [4096], replicated, may hold values from 0 to 255
- coef_income: int32 [4096], replicated, may hold values from 0 to 63
- owner: int32 [4096], replicated, may hold values from 0 to 7, as said below
Outputs:
- reduced: float32 [32, 8192], P(('grp', 'col'), ('wide', 'inc')), parts along dimension 0
There are 2 independent parts, one for each index of `grp`. A program takes and returns all parts, laid end to end along the dimension named above; an argument that names none is the same for every part. Nothing has to cross between parts.
Inputs may be any that keep to these rules, and one draw needn't show every extreme that they name: `coef_liquid`: every retained coefficient has liquid frequency below 128. No owner has more than 1024 rows, and some owner has exactly 1024.
All inputs are finite; a program needn't handle non-finite values. No bound on the sum of `mask_liquid` or of `mask_illiquid` on one device may be relied on, other than what follows from the above.
Results may differ from a plain program's by a relative error of at most 0.0003.
Values may be sent and summed in bfloat16 or wider, within the bound.
No kernel may reach another device: no remote copies, remote signals or barrier semaphores. Data moves between devices by JAX's collectives and lax.ppermute only.
A program may use at most 256 MiB of HBM per device.

v0:
```python
import jax
import jax.numpy as jnp
from jax import lax
from jax.sharding import PartitionSpec as P

NB = 512
NA = 256
NZ = 64
KBLOW = 128


def padded_2(cells, sides, width):
    for axis, dim in sides:
        count = lax.axis_size(axis)
        ends = count - 1
        head = lax.slice_in_dim(cells, 0, width, axis=dim)
        tail = lax.slice_in_dim(cells, cells.shape[dim] - width, cells.shape[dim], axis=dim)
        cells = jnp.concatenate(
            [
                lax.ppermute(tail, axis, [(i, (i + 1) % count) for i in range(ends)]),
                cells,
                lax.ppermute(head, axis, [((i + 1) % count, i) for i in range(ends)]),
            ],
            axis=dim,
        )
    return cells


def cosine_table(count):
    freq = jnp.arange(count, dtype=jnp.int32)[:, None]
    cell = jnp.arange(count, dtype=jnp.int32)[None, :]
    phase = (2 * cell + 1) * freq % (4 * count)
    angle = jnp.pi * phase.astype(jnp.float32) / (2.0 * count)
    first = jnp.where(freq == 0, jnp.sqrt(jnp.float32(0.5)), jnp.float32(1.0))
    return jnp.cos(angle) * jnp.sqrt(jnp.float32(2.0 / count)) * first


def slot_targets(owner, owners, capacity):
    onehot = (owner[:, None] == jnp.arange(owners, dtype=jnp.int32)[None, :]).astype(jnp.int32)
    before = jnp.cumsum(onehot, axis=0) - onehot
    slot = jnp.sum(before * onehot, axis=1)
    return owner * capacity + slot


def body(
    values_in,
    shock_load,
    price_field,
    rate_liquid,
    rate_illiquid,
    mask_liquid,
    mask_illiquid,
    jump_inverse,
    coef_liquid,
    coef_illiquid,
    coef_income,
    owner,
):
    high = lax.Precision.HIGH
    columns, nz_loc, na_loc, _ = values_in.shape
    wide_pos = lax.axis_index("wide")
    inc_pos = lax.axis_index("inc")
    wide_count = lax.axis_size("wide")
    padded = padded_2(values_in, (("wide", 2),), 1).astype(jnp.float32)
    center = padded[:, :, 1:-1]
    lower = jnp.where(wide_pos == 0, center[:, :, 0:1], padded[:, :, 0:1])
    upper = jnp.where(wide_pos == wide_count - 1, center[:, :, -1:], padded[:, :, -1:])
    fwd_a = jnp.concatenate([center[:, :, 1:], upper], axis=2) - center
    bwd_a = center - jnp.concatenate([lower, center[:, :, :-1]], axis=2)
    step_b = center[:, :, :, 1:] - center[:, :, :, :-1]
    zero_b = jnp.zeros(center.shape[:3] + (1,), jnp.float32)
    fwd_b = jnp.concatenate([step_b, zero_b], axis=3)
    bwd_b = jnp.concatenate([zero_b, step_b], axis=3)
    mask_b = mask_liquid.astype(jnp.float32)
    mask_a = mask_illiquid.astype(jnp.float32)
    load = shock_load[:, None, None, None]
    explicit = (
        center
        + rate_liquid * (mask_b * fwd_b - (1.0 - mask_b) * bwd_b)
        + rate_illiquid * (mask_a * fwd_a - (1.0 - mask_a) * bwd_a)
        + load * price_field
    )
    table_b = cosine_table(NB)[:KBLOW]
    liquid_part = jnp.einsum("kb,czab->czak", table_b, explicit, precision=high)
    table_a = lax.dynamic_slice_in_dim(cosine_table(NA), wide_pos * na_loc, na_loc, axis=1)
    illiquid_part = jnp.einsum("ja,czak->jkcz", table_a, liquid_part, precision=high)
    rows = illiquid_part.reshape(NA * KBLOW, columns * nz_loc)
    picked = jnp.take(rows, coef_illiquid * KBLOW + coef_liquid, axis=0)
    folded = jnp.dot(cosine_table(NZ), jump_inverse, precision=lax.Precision.HIGHEST)
    folded = lax.dynamic_slice_in_dim(folded, inc_pos * nz_loc, nz_loc, axis=1)
    weight = jnp.take(folded, coef_income, axis=0)
    partial = jnp.sum(picked.reshape(-1, columns, nz_loc) * weight[:, None, :], axis=2)
    kept = lax.psum(partial, ("wide", "inc"))
    owners = lax.axis_size(("wide", "inc"))
    count = owner.shape[0]
    capacity = 2 * count // owners
    targets = slot_targets(owner, owners, capacity)
    source = (
        jnp.full((owners * capacity,), count, jnp.int32)
        .at[targets]
        .set(jnp.arange(count, dtype=jnp.int32))
    )
    mine = lax.dynamic_slice_in_dim(source, lax.axis_index(("wide", "inc")) * capacity, capacity)
    gathered = jnp.take(kept, jnp.minimum(mine, count - 1), axis=0)
    return jnp.where((mine < count)[None, :], gathered.T, jnp.float32(0.0))


def solution(mesh):
    placed = (
        P(("grp", "col"), "inc", "wide", None),
        P(("grp", "col")),
        P(("grp", "inc"), "wide", None),
        P(("grp", "inc"), "wide", None),
        P(("grp", "inc"), "wide", None),
        P(("grp", "inc"), "wide", None),
        P(("grp", "inc"), "wide", None),
        P("grp", None),
        P(),
        P(),
        P(),
        P(),
    )
    return jax.shard_map(
        body,
        mesh=mesh,
        in_specs=placed,
        out_specs=P(("grp", "col"), ("wide", "inc")),
        check_vma=False,
    )
```

profile of v0, /device:TPU:0, one launch (start us, length us, event | category | flops | bytes accessed | tf_op | source)
XLA Modules:
  0.0 500.5 jit_solution(14844286475312916411)
XLA Ops:
  6.6 3.3 fusion.94
  9.9 5.6 %collective-permute-start = (bf16[8,32,1,512]{3,1,2,0:T(8,128)(2,1)S(1)}, bf16[8,32,1,512]{3,1,2,0:T(8,128)(2,1)}, u32[]{:S(2)}, u32[]{:S(2)}) collective-permute-start(bf16[8,32,1,512]{3,1,2,0:T(8,128)(2,1)S(1)} %copy.34), channel_id=1, source_target_pairs={{0,4},{4,8},{8,12},{1,5},{5,9},{9,13},{2,6},{6,10},{10,14},{3,7},{... | collective-permute-start | bytes 786440 | tf_op jit(solution)/shard_map/ppermute | solution.py:20
  15.6 0.7 copy.35
  16.3 1.3 collective-permute-start.1
  17.6 4.9 convert_element_type.28
  22.6 8.5 %broadcast_subtract_fusion = (f32[32,64,512]{2,1,0:T(8,128)}, f32[32,64,512]{2,1,0:T(8,128)}) fusion(s32[32,64,512]{2,1,0:T(8,128)} %param.18, s32[32,64,512]{2,1,0:T(8,128)} %param.17), kind=kLoop, calls=%fused_computation.39 | loop fusion | flops 4194304 | bytes 16777216 | tf_op jit(solution)/shard_map/sub | solution.py:80
  31.1 4.9 convert_element_type.29
  36.0 0.8 broadcast_compare_fusion.3
  36.9 0.9 negate_select_fusion.2
  40.3 14.1 %gather_fusion.1 = f32[4096,32]{1,0:T(8,128)} fusion(f32[64,32]{1,0:T(8,128)S(1)} %copy.28, s32[4096]{0:T(1024)S(1)} %fusion.78), kind=kCustom, calls=%fused_computation.1 | custom fusion | bytes 1064960 | tf_op jit(solution)/shard_map/jit(_take)/gather | solution.py:91
  54.4 3.6 broadcast_select_fusion
  58.0 1.4 copy.29
  59.4 2.3 reduce-window.6
  62.5 15.5 %scatter_custom_fusion = s32[8192]{0:T(1024)S(1)} fusion(s32[4096]{0:T(1024)S(1)} %compare_select_fusion.2, s32[4096]{0:T(1024)S(1)} %iota.47, s32[]{:T(128)} %constant.66.clone.1), kind=kCustom, calls=%fused_computation.109 | custom fusion | bytes 32772 | tf_op jit(solution)/shard_map/scatter | solution.py:101
  79.2 1.4 copy.23
  80.6 1.4 copy.24
  82.0 20.9 %maximum_convert_fusion = f32[8,32,66,512]{3,2,1,0:T(8,128)} fusion(bf16[8,32,1,512]{3,2,1,0:T(2,128)(2,1)S(1)} %copy.24, bf16[8,32,64,512]{3,2,1,0:T(8,128)(2,1)} %param.12, bf16[8,32,1,512]{3,2,1,0:T(2,128)(2,1)S(1)} %copy.23), kind=kLoop, calls=%fused_computation.28 | loop fusion | flops 51904512 | bytes 51904512 | tf_op jit(solution)/shard_map/convert_element_type | solution.py:64
  102.9 47.7 %fusion.93 = (f32[8,32,63,512]{3,2,1,0:T(8,128)}, f32[8,32,63,512]{3,2,1,0:T(8,128)}) fusion(f32[8,32,66,512]{3,2,1,0:T(8,128)} %maximum_convert_fusion), kind=kLoop, calls=%fused_computation.140 | loop fusion | bytes 132120576 | tf_op jit(solution)/shard_map/slice | solution.py:69
  150.6 36.7 %slice_subtract_fusion = f32[8,32,64,511]{3,2,1,0:T(8,128)} fusion(f32[8,32,66,512]{3,2,1,0:T(8,128)} %maximum_convert_fusion), kind=kLoop, calls=%fused_computation.5 | loop fusion | flops 8372224 | bytes 100466688 | tf_op jit(solution)/shard_map/sub | solution.py:70
  187.3 4.8 broadcast_select_fusion.1
  192.2 73.0 %fusion.5 = f32[8,32,64,128]{3,2,1,0:T(8,128)} fusion(f32[8,32,1,512]{3,2,1,0:T(1,128)S(1)} %get-tuple-element.8, f32[8,32,63,512]{3,2,1,0:T(8,128)} %get-tuple-element.6, f32[8,32,63,512]{3,2,1,0:T(8,128)} %get-tuple-element.5, f32[8,32,1,512]{3,2,1,0:T(1,128)S(1)} %get-tuple-element.7, f32[8,32,66,512]{3,2,1,0:T(8,128)} %maximum_convert_fusion, ...), kind=kOutput, calls=%fused_computation.12 | convolution fusion | flops 6577061888 | bytes 173409280 | tf_op jit(solution)/shard_map/kb,czab->czak/dot_general | solution.py:84
  265.2 22.0 %convolution_bitcast_fusion = f32[256,128,8,32]{0,1,3,2:T(8,128)} fusion(f32[8,32,64,128]{3,2,1,0:T(8,128)} %fusion.5, s32[256,256]{0,1:T(8,128)} %negate_select_fusion.2, s32[]{:T(128)S(6)} %select_n.124, pred[256,256]{0,1:T(32,128)(4,1)} %get-tuple-element.16, pred[256,256]{0,1:T(32,128)(4,1)} %get-tuple-element.15, f32[256]{0:T(256)S(1)} %copy-done.14), kind=kOutput, calls=%fused_computation.37 | convolution fusion | flops 3221323776 | bytes 42042372 | tf_op jit(solution)/shard_map/ja,czak->jkcz/dot_general | solution.py:86
  287.3 31.1 %copy.25 = f32[256,128,8,32]{1,0,3,2:T(8,128)} copy(f32[256,128,8,32]{0,1,3,2:T(8,128)} %convolution_bitcast_fusion) | data formatting | bytes 67108864 | tf_op jit(solution)/shard_map/ja,czak->jkcz/transpose | solution.py:86
  318.4 31.8 %copy.40 = f32[32,8,256,128]{3,1,2,0:T(8,128)} copy(f32[32,8,256,128]{3,2,1,0:T(8,128)} %bitcast.48) | data formatting | bytes 67108864
  350.1 33.4 %copy.26 = f32[32768,256]{1,0:T(8,128)} copy(f32[32768,256]{0,1:T(8,128)} %bitcast.49) | data formatting | bytes 67108864 | tf_op jit(solution)/shard_map/reshape | solution.py:87
  383.6 26.7 %gather_fusion = f32[4096,256]{1,0:T(8,128)} fusion(f32[32768,256]{1,0:T(8,128)} %copy.26, s32[4096]{0:T(1024)S(1)} %copy-done.5), kind=kCustom, calls=%fused_computation | custom fusion | bytes 8404992 | tf_op jit(solution)/shard_map/jit(_take)/gather | solution.py:88
  410.3 5.6 %copy.27 = f32[4096,256]{0,1:T(8,128)} copy(f32[4096,256]{1,0:T(8,128)} %gather_fusion) | data formatting | bytes 8388608 | tf_op jit(solution)/shard_map/jit(_take)/gather | solution.py:88
  415.9 2.9 multiply_reduce_fusion
  418.8 1.9 copy.30
  421.5 66.6 %all-reduce.4.cloned.1.call-done = f32[4096,8]{1,0:T(8,128)} async-done(((f32[4096,8]{1,0:T(8,128)}), f32[4096,8]{1,0:T(8,128)}) %all-reduce.4.cloned.1.call-update) | async-done | bytes 131088 | tf_op jit(solution)/shard_map/psum | solution.py:93
  488.1 4.4 gather_fusion.2
  492.8 0.8 copy.31
  (62 shorter events, 5.6 us)
Async XLA Ops:
  6.5 33.3 %copy-start = (f32[64,64]{1,0:T(8,128)S(1)}, f32[64,64]{1,0:T(8,128)}, u32[]{:S(2)}) copy-start(f32[64,64]{1,0:T(8,128)} %param.19) | copy-start | bytes 49156
  6.5 31.8 %copy-start.8 = (s32[4096]{0:T(1024)S(1)}, s32[4096]{0:T(1024)}, u32[]{:S(2)}) copy-start(s32[4096]{0:T(1024)} %param.22) | copy-start | bytes 49156
  6.5 31.8 %copy-start.6 = (s32[4096]{0:T(1024)S(1)}, s32[4096]{0:T(1024)}, u32[]{:S(2)}) copy-start(s32[4096]{0:T(1024)} %param.20) | copy-start | bytes 49156
  6.5 31.8 %copy-start.7 = (s32[4096]{0:T(1024)S(1)}, s32[4096]{0:T(1024)}, u32[]{:S(2)}) copy-start(s32[4096]{0:T(1024)} %param.21) | copy-start | bytes 49156
  6.5 52.9 %copy-start.4 = (s32[4096]{0:T(1024)S(1)}, s32[4096]{0:T(1024)}, u32[]{:S(2)}) copy-start(s32[4096]{0:T(1024)} %param.23) | copy-start | bytes 49156
  6.5 481.5 %all-reduce.4.cloned.1.call-start = ((), (), s32[]{:S(2)}) async-start(), calls=%async_computation | async-start | bytes 4194304 | tf_op jit(solution)/shard_map/psum | solution.py:93
  9.9 69.3 %collective-permute-start = (bf16[8,32,1,512]{3,1,2,0:T(8,128)(2,1)S(1)}, bf16[8,32,1,512]{3,1,2,0:T(8,128)(2,1)}, u32[]{:S(2)}, u32[]{:S(2)}) collective-permute-start(bf16[8,32,1,512]{3,1,2,0:T(8,128)(2,1)S(1)} %copy.34), channel_id=1, source_target_pairs={{0,4},{4,8},{8,12},{1,5},{5,9},{9,13},{2,6},{6,10},{10,14},{3,7},{... | collective-permute-start | bytes 786440 | tf_op jit(solution)/shard_map/ppermute | solution.py:20
  16.3 64.3 %collective-permute-start.1 = (bf16[8,32,1,512]{3,1,2,0:T(8,128)(2,1)}, bf16[8,32,1,512]{3,1,2,0:T(8,128)(2,1)}, u32[]{:S(2)}, u32[]{:S(2)}) collective-permute-start(bf16[8,32,1,512]{3,1,2,0:T(8,128)(2,1)} %copy.35), channel_id=1, source_target_pairs={{4,0},{8,4},{12,8},{5,1},{9,5},{13,9},{6,2},{10,6},{14,10},{7,3},{... | collective-permute-start | bytes 786440 | tf_op jit(solution)/shard_map/ppermute | solution.py:22
  36.0 66.9 %copy-start.13 = (f32[512]{0:T(512)}, f32[512]{0:T(512)S(1)}, u32[]{:S(2)}) copy-start(f32[512]{0:T(512)S(1)} %select_multiply_fusion) | copy-start | bytes 6148
  78.0 72.6 %copy-start.9 = (s32[8192]{0:T(1024)}, s32[8192]{0:T(1024)S(1)}, u32[]{:S(2)}) copy-start(s32[8192]{0:T(1024)S(1)} %scatter_custom_fusion) | copy-start | bytes 98308
  150.6 41.6 %copy-start.10 = (f32[8]{0:T(128)S(1)}, f32[8]{0:T(128)}, u32[]{:S(2)}) copy-start(f32[8]{0:T(128)} %param.13) | copy-start | bytes 100
  150.6 41.6 %slice-start = ((f32[512]{0:T(512)}), f32[128]{0:T(128)S(1)}, s32[]{:S(2)}) async-start(f32[512]{0:T(512)} %copy-done.13), calls=%async_computation.1 | async-start | bytes 1024 | tf_op jit(solution)/shard_map/slice | solution.py:83
  187.3 4.9 copy-start.2
  192.2 73.0 %copy-start.14 = (f32[256]{0:T(256)S(1)}, f32[256]{0:T(256)}, u32[]{:S(2)}) copy-start(f32[256]{0:T(256)} %fusion.80) | copy-start | bytes 3076
  350.1 33.4 %copy-start.5 = (s32[4096]{0:T(1024)S(1)}, s32[4096]{0:T(1024)}, u32[]{:S(2)}) copy-start(s32[4096]{0:T(1024)} %broadcast_clamp_fusion) | copy-start | bytes 49156
  350.1 143.5 %copy-start.1 = (f32[64,64]{1,0:T(8,128)S(1)}, f32[64,64]{1,0:T(8,128)}, u32[]{:S(2)}) copy-start(f32[64,64]{1,0:T(8,128)} %param.19) | copy-start | bytes 49156
  383.6 32.3 %copy-start.3 = (f32[4096,32]{0,1:T(8,128)S(1)}, f32[4096,32]{0,1:T(8,128)}, u32[]{:S(2)}) copy-start(f32[4096,32]{0,1:T(8,128)} %copy.29) | copy-start | bytes 1572868
  383.6 32.3 %copy-start.11 = (pred[4096]{0:T(1024)(128)(4,1)S(1)}, pred[4096]{0:T(1024)(128)(4,1)}, u32[]{:S(2)}) copy-start(pred[4096]{0:T(1024)(128)(4,1)} %compare_and_fusion.1) | copy-start | bytes 12292
  383.6 104.5 %copy-start.12 = (s32[1024]{0:T(1024)S(1)}, s32[1024]{0:T(1024)}, u32[]{:S(2)}) copy-start(s32[1024]{0:T(1024)} %fusion.79) | copy-start | bytes 12292
Sparse Core Ops, SparseCore 0:
  420.9 67.1 all-reduce.3
where the time goes:
time: 502 us; the launch traced here: 500 us
  local copies, waits for them, and re-layouts  222 us (44%)
  other arithmetic  96.1 us (19%)
  matrix products  95.4 us (19%)
  waiting for transfers between devices  66.7 us (13%)
  between operations  13.7 us (3%)
  starting transfers between devices  6.96 us (1%)
    dot_general x1, matrix products, body(): liquid_part = jnp.einsum('kb,czab->czak', table_b, explicit, precision=high)  73 us
    psum x1, waiting for transfers between devices, body(): kept = lax.psum(partial, ('wide', 'inc'))  66.6 us
    slice x1, local copies, waits for them, and re-layouts, body(): bwd_a = center - jnp.concatenate([lower, center[:, :, :-1]], axis=2)  47.7 us
    sub x1, other arithmetic, body(): step_b = center[:, :, :, 1:] - center[:, :, :, :-1]  36.7 us
    reshape x1, local copies, waits for them, and re-layouts, body(): rows = illiquid_part.reshape(NA * KBLOW, columns * nz_loc)  33.4 us
    unnamed x33, local copies, waits for them, and re-layouts  32.6 us
    gather x2, local copies, waits for them, and re-layouts, body(): picked = jnp.take(rows, coef_illiquid * KBLOW + coef_liquid, axis=0)  32.3 us
    transpose x1, local copies, waits for them, and re-layouts, body(): jnp.einsum('ja,czak->jkcz', table_a, liquid_part, precision=high)  31.1 us
  transfers between devices with their start and end apart: 3, of which 1 were waited for; matrix products, arithmetic and copies ran while one was open for 13% of the time, Pallas kernels for 0%

commit v1 on v0

--- a/solution.py
+++ b/solution.py
@@ -90,7 +90,7 @@
     folded = lax.dynamic_slice_in_dim(folded, inc_pos * nz_loc, nz_loc, axis=1)
     weight = jnp.take(folded, coef_income, axis=0)
     partial = jnp.sum(picked.reshape(-1, columns, nz_loc) * weight[:, None, :], axis=2)
-    kept = lax.psum(partial, ("wide", "inc"))
+    kept = lax.psum(lax.psum(partial, "inc"), "wide")
     owners = lax.axis_size(("wide", "inc"))
     count = owner.shape[0]
     capacity = 2 * count // owners

time: 502 us -> 531 us (1.058)
  waiting for transfers between devices: 66.7 us -> 98.2 us
    psum x1 -> x2, waiting for transfers between devices: 66.6 us -> 98.2 us  [body(): kept = lax.psum(lax.psum(partial, 'inc'), 'wide')]
    unnamed x33 -> x35, local copies, waits for them, and re-layouts: 32.6 us -> 32.6 us
  transfers between devices with their start and end apart: 3 -> 4, of which waited for: 1 -> 2; matrix products, arithmetic and copies ran while one was open for 13% -> 12% of each run, Pallas kernels for 0% -> 0%
where the time goes in v1:
time: 531 us; the launch traced here: 529 us
  local copies, waits for them, and re-layouts  222 us (42%)
  waiting for transfers between devices  98.2 us (18%)
  matrix products  95.3 us (18%)
  other arithmetic  92.9 us (17%)
  between operations  13.7 us (3%)
  starting transfers between devices  6.99 us (1%)
    psum x2, waiting for transfers between devices, body(): kept = lax.psum(lax.psum(partial, 'inc'), 'wide')  98.2 us
    dot_general x1, matrix products, body(): liquid_part = jnp.einsum('kb,czab->czak', table_b, explicit, precision=high)  73.2 us
    slice x1, local copies, waits for them, and re-layouts, body(): bwd_a = center - jnp.concatenate([lower, center[:, :, :-1]], axis=2)  47.7 us
    sub x1, other arithmetic, body(): step_b = center[:, :, :, 1:] - center[:, :, :, :-1]  36.7 us
    reshape x1, local copies, waits for them, and re-layouts, body(): rows = illiquid_part.reshape(NA * KBLOW, columns * nz_loc)  33.5 us
    unnamed x35, local copies, waits for them, and re-layouts  32.6 us
    gather x2, local copies, waits for them, and re-layouts, body(): picked = jnp.take(rows, coef_illiquid * KBLOW + coef_liquid, axis=0)  32.4 us
    transpose x1, local copies, waits for them, and re-layouts, body(): jnp.einsum('ja,czak->jkcz', table_a, liquid_part, precision=high)  31 us
  transfers between devices with their start and end apart: 4, of which 2 were waited for; matrix products, arithmetic and copies ran while one was open for 12% of the time, Pallas kernels for 0%

profile of v1, /device:TPU:0, one launch (start us, length us, event | category | flops | bytes accessed | tf_op | source)
XLA Modules:
  0.0 529.2 jit_solution(7804463718786950346)
XLA Ops:
  6.6 3.4 fusion.94
  10.1 5.6 %collective-permute-start = (bf16[8,32,1,512]{3,1,2,0:T(8,128)(2,1)S(1)}, bf16[8,32,1,512]{3,1,2,0:T(8,128)(2,1)}, u32[]{:S(2)}, u32[]{:S(2)}) collective-permute-start(bf16[8,32,1,512]{3,1,2,0:T(8,128)(2,1)S(1)} %copy.34), channel_id=1, source_target_pairs={{0,4},{4,8},{8,12},{1,5},{5,9},{9,13},{2,6},{6,10},{10,14},{3,7},{... | collective-permute-start | bytes 786440 | tf_op jit(solution)/shard_map/ppermute | solution.py:20
  16.5 1.3 collective-permute-start.1
  17.8 4.9 convert_element_type.28
  22.7 8.5 %broadcast_subtract_fusion = (f32[32,64,512]{2,1,0:T(8,128)}, f32[32,64,512]{2,1,0:T(8,128)}) fusion(s32[32,64,512]{2,1,0:T(8,128)} %param.18, s32[32,64,512]{2,1,0:T(8,128)} %param.17), kind=kLoop, calls=%fused_computation.39 | loop fusion | flops 4194304 | bytes 16777216 | tf_op jit(solution)/shard_map/sub | solution.py:80
  31.2 2.5 convert_element_type.29
  33.7 0.9 broadcast_compare_fusion.3
  34.6 0.9 negate_select_fusion.2
  38.0 14.2 %gather_fusion.1 = f32[4096,32]{1,0:T(8,128)} fusion(f32[64,32]{1,0:T(8,128)S(1)} %copy.28, s32[4096]{0:T(1024)S(1)} %fusion.78), kind=kCustom, calls=%fused_computation.1 | custom fusion | bytes 1064960 | tf_op jit(solution)/shard_map/jit(_take)/gather | solution.py:91
  52.2 3.6 broadcast_select_fusion
  55.8 1.4 copy.29
  57.2 2.3 reduce-window.6
  61.4 1.4 copy.23
  62.8 1.4 copy.24
  64.2 20.8 %maximum_convert_fusion = f32[8,32,66,512]{3,2,1,0:T(8,128)} fusion(bf16[8,32,1,512]{3,2,1,0:T(2,128)(2,1)S(1)} %copy.24, bf16[8,32,64,512]{3,2,1,0:T(8,128)(2,1)} %param.12, bf16[8,32,1,512]{3,2,1,0:T(2,128)(2,1)S(1)} %copy.23), kind=kLoop, calls=%fused_computation.28 | loop fusion | flops 51904512 | bytes 51904512 | tf_op jit(solution)/shard_map/convert_element_type | solution.py:64
  85.0 47.7 %fusion.93 = (f32[8,32,63,512]{3,2,1,0:T(8,128)}, f32[8,32,63,512]{3,2,1,0:T(8,128)}) fusion(f32[8,32,66,512]{3,2,1,0:T(8,128)} %maximum_convert_fusion), kind=kLoop, calls=%fused_computation.140 | loop fusion | bytes 132120576 | tf_op jit(solution)/shard_map/slice | solution.py:69
  132.7 36.7 %slice_subtract_fusion = f32[8,32,64,511]{3,2,1,0:T(8,128)} fusion(f32[8,32,66,512]{3,2,1,0:T(8,128)} %maximum_convert_fusion), kind=kLoop, calls=%fused_computation.5 | loop fusion | flops 8372224 | bytes 100466688 | tf_op jit(solution)/shard_map/sub | solution.py:70
  169.4 4.9 broadcast_select_fusion.1
  174.3 73.2 %fusion.5 = f32[8,32,64,128]{3,2,1,0:T(8,128)} fusion(f32[8,32,1,512]{3,2,1,0:T(1,128)S(1)} %get-tuple-element.8, f32[8,32,63,512]{3,2,1,0:T(8,128)} %get-tuple-element.6, f32[8,32,63,512]{3,2,1,0:T(8,128)} %get-tuple-element.5, f32[8,32,1,512]{3,2,1,0:T(1,128)S(1)} %get-tuple-element.7, f32[8,32,66,512]{3,2,1,0:T(8,128)} %maximum_convert_fusion, ...), kind=kOutput, calls=%fused_computation.12 | convolution fusion | flops 6577061888 | bytes 173409280 | tf_op jit(solution)/shard_map/kb,czab->czak/dot_general | solution.py:84
  247.5 21.8 %convolution_bitcast_fusion = f32[256,128,8,32]{0,1,3,2:T(8,128)} fusion(f32[8,32,64,128]{3,2,1,0:T(8,128)} %fusion.5, s32[256,256]{0,1:T(8,128)} %negate_select_fusion.2, s32[]{:T(128)S(6)} %select_n.124, pred[256,256]{0,1:T(32,128)(4,1)} %get-tuple-element.16, pred[256,256]{0,1:T(32,128)(4,1)} %get-tuple-element.15, f32[256]{0:T(256)S(1)} %copy-done.15), kind=kOutput, calls=%fused_computation.37 | convolution fusion | flops 3221323776 | bytes 42042372 | tf_op jit(solution)/shard_map/ja,czak->jkcz/dot_general | solution.py:86
  269.3 31.0 %copy.25 = f32[256,128,8,32]{1,0,3,2:T(8,128)} copy(f32[256,128,8,32]{0,1,3,2:T(8,128)} %convolution_bitcast_fusion) | data formatting | bytes 67108864 | tf_op jit(solution)/shard_map/ja,czak->jkcz/transpose | solution.py:86
  300.4 31.7 %copy.40 = f32[32,8,256,128]{3,1,2,0:T(8,128)} copy(f32[32,8,256,128]{3,2,1,0:T(8,128)} %bitcast.48) | data formatting | bytes 67108864
  332.1 33.5 %copy.26 = f32[32768,256]{1,0:T(8,128)} copy(f32[32768,256]{0,1:T(8,128)} %bitcast.49) | data formatting | bytes 67108864 | tf_op jit(solution)/shard_map/reshape | solution.py:87
  365.6 26.8 %gather_fusion = f32[4096,256]{1,0:T(8,128)} fusion(f32[32768,256]{1,0:T(8,128)} %copy.26, s32[4096]{0:T(1024)S(1)} %copy-done.7), kind=kCustom, calls=%fused_computation | custom fusion | bytes 8404992 | tf_op jit(solution)/shard_map/jit(_take)/gather | solution.py:88
  392.4 5.6 %copy.27 = f32[4096,256]{0,1:T(8,128)} copy(f32[4096,256]{1,0:T(8,128)} %gather_fusion) | data formatting | bytes 8388608 | tf_op jit(solution)/shard_map/jit(_take)/gather | solution.py:88
  398.0 2.9 multiply_reduce_fusion
  400.9 1.9 copy.30
  403.0 15.5 %scatter_custom_fusion = s32[8192]{0:T(1024)S(1)} fusion(s32[4096]{0:T(1024)S(1)} %compare_select_fusion.2, s32[4096]{0:T(1024)S(1)} %iota.47, s32[]{:T(128)} %constant.66.clone.1), kind=kCustom, calls=%fused_computation.109 | custom fusion | bytes 32772 | tf_op jit(solution)/shard_map/scatter | solution.py:101
  418.5 8.1 %all-reduce.5.cloned.1.call-done = f32[4096,8]{1,0:T(8,128)} async-done(((f32[4096,8]{1,0:T(8,128)}), f32[4096,8]{1,0:T(8,128)}) %all-reduce.5.cloned.1.call-update) | async-done | bytes 131088 | tf_op jit(solution)/shard_map/psum | solution.py:93
  426.7 90.1 %all-reduce.7.cloned.1.call-done = f32[4096,8]{1,0:T(8,128)} async-done(((f32[4096,8]{1,0:T(8,128)}), f32[4096,8]{1,0:T(8,128)}) %all-reduce.7.cloned.1.call-update) | async-done | bytes 131088 | tf_op jit(solution)/shard_map/psum | solution.py:93
  516.8 4.4 gather_fusion.2
  521.6 0.8 copy.31
  (67 shorter events, 5.7 us)
Async XLA Ops:
  6.5 31.0 %copy-start = (f32[64,64]{1,0:T(8,128)S(1)}, f32[64,64]{1,0:T(8,128)}, u32[]{:S(2)}) copy-start(f32[64,64]{1,0:T(8,128)} %param.19) | copy-start | bytes 49156
  6.5 29.5 %copy-start.11 = (s32[4096]{0:T(1024)S(1)}, s32[4096]{0:T(1024)}, u32[]{:S(2)}) copy-start(s32[4096]{0:T(1024)} %param.22) | copy-start | bytes 49156
  6.5 29.5 %copy-start.9 = (s32[4096]{0:T(1024)S(1)}, s32[4096]{0:T(1024)}, u32[]{:S(2)}) copy-start(s32[4096]{0:T(1024)} %param.20) | copy-start | bytes 49156
  6.5 29.6 %copy-start.10 = (s32[4096]{0:T(1024)S(1)}, s32[4096]{0:T(1024)}, u32[]{:S(2)}) copy-start(s32[4096]{0:T(1024)} %param.21) | copy-start | bytes 49156
  6.5 420.1 %all-reduce.5.cloned.1.call-start = ((), (), s32[]{:S(2)}) async-start(), calls=%async_computation | async-start | bytes 4194304 | tf_op jit(solution)/shard_map/psum | solution.py:93
  6.6 24.6 %copy-start.3 = (s32[32,64,512]{2,1,0:T(8,128)S(1)}, s32[32,64,512]{2,1,0:T(8,128)}, u32[]{:S(2)}) copy-start(s32[32,64,512]{2,1,0:T(8,128)} %param.18) | copy-start | bytes 12582916
  10.1 51.4 %collective-permute-start = (bf16[8,32,1,512]{3,1,2,0:T(8,128)(2,1)S(1)}, bf16[8,32,1,512]{3,1,2,0:T(8,128)(2,1)}, u32[]{:S(2)}, u32[]{:S(2)}) collective-permute-start(bf16[8,32,1,512]{3,1,2,0:T(8,128)(2,1)S(1)} %copy.34), channel_id=1, source_target_pairs={{0,4},{4,8},{8,12},{1,5},{5,9},{9,13},{2,6},{6,10},{10,14},{3,7},{... | collective-permute-start | bytes 786440 | tf_op jit(solution)/shard_map/ppermute | solution.py:20
  16.5 46.4 %collective-permute-start.1 = (bf16[8,32,1,512]{3,1,2,0:T(8,128)(2,1)}, bf16[8,32,1,512]{3,1,2,0:T(8,128)(2,1)}, u32[]{:S(2)}, u32[]{:S(2)}) collective-permute-start(bf16[8,32,1,512]{3,1,2,0:T(8,128)(2,1)} %copy.35), channel_id=1, source_target_pairs={{4,0},{8,4},{12,8},{5,1},{9,5},{13,9},{6,2},{10,6},{14,10},{7,3},{... | collective-permute-start | bytes 786440 | tf_op jit(solution)/shard_map/ppermute | solution.py:22
  31.2 26.0 %copy-start.5 = (s32[4096]{0:T(1024)S(1)}, s32[4096]{0:T(1024)}, u32[]{:S(2)}) copy-start(s32[4096]{0:T(1024)} %param.23) | copy-start | bytes 49156
  33.7 51.3 %copy-start.14 = (f32[512]{0:T(512)}, f32[512]{0:T(512)S(1)}, u32[]{:S(2)}) copy-start(f32[512]{0:T(512)S(1)} %select_multiply_fusion) | copy-start | bytes 6148
  169.4 4.9 copy-start.2
  169.4 4.9 copy-start.12
  169.4 4.9 slice-start
  174.3 73.2 %copy-start.15 = (f32[256]{0:T(256)S(1)}, f32[256]{0:T(256)}, u32[]{:S(2)}) copy-start(f32[256]{0:T(256)} %fusion.80) | copy-start | bytes 3076
  332.1 33.5 %copy-start.7 = (s32[4096]{0:T(1024)S(1)}, s32[4096]{0:T(1024)}, u32[]{:S(2)}) copy-start(s32[4096]{0:T(1024)} %broadcast_clamp_fusion) | copy-start | bytes 49156
  365.6 32.5 %copy-start.4 = (f32[4096,32]{0,1:T(8,128)S(1)}, f32[4096,32]{0,1:T(8,128)}, u32[]{:S(2)}) copy-start(f32[4096,32]{0,1:T(8,128)} %copy.29) | copy-start | bytes 1572868
  365.6 32.5 %copy-start.13 = (pred[4096]{0:T(1024)(128)(4,1)S(1)}, pred[4096]{0:T(1024)(128)(4,1)}, u32[]{:S(2)}) copy-start(pred[4096]{0:T(1024)(128)(4,1)} %compare_and_fusion.1) | copy-start | bytes 12292
  365.6 37.4 %copy-start.6 = (s32[4096]{0:T(1024)S(1)}, s32[4096]{0:T(1024)}, u32[]{:S(2)}) copy-start(s32[4096]{0:T(1024)} %param.23) | copy-start | bytes 49156
  365.6 37.4 %copy-start.8 = (s32[4096]{0:T(1024)S(1)}, s32[4096]{0:T(1024)}, u32[]{:S(2)}) copy-start(s32[4096]{0:T(1024)} %fusion.42) | copy-start | bytes 49156
  365.6 156.8 %copy-start.1 = (f32[64,64]{1,0:T(8,128)S(1)}, f32[64,64]{1,0:T(8,128)}, u32[]{:S(2)}) copy-start(f32[64,64]{1,0:T(8,128)} %param.19) | copy-start | bytes 49156
  402.9 113.9 %all-reduce.7.cloned.1.call-start = ((), (), s32[]{:S(2)}) async-start(), calls=%async_computation.1 | async-start | bytes 4194304 | tf_op jit(solution)/shard_map/psum | solution.py:93
Sparse Core Ops, SparseCore 0:
  403.0 23.5 all-reduce.4
  429.1 87.6 all-reduce.6
